TPU v7x, 128 devices: a whole 4x4x4 slice. The times are simulated.
128 devices in a mesh: grp: 8 (over x_hi, z), vocab: 16 (over y, x_lo, core).
Axes of the slice: x: 4 (x_hi: 2, x_lo: 2; x = x_hi * 2 + x_lo), y: 4, z: 4, core: 2. Of those that a mesh axis runs over, the one named last changes fastest.
Arguments:
- hidden: bfloat16 [1024, 8192], P('grp', 'vocab')
- head_weight: bfloat16 [81920, 8192], P(('grp', 'vocab'))
- targets: int32 [1024], replicated, may hold values from 0 to 81919
- old_logprobs: float32 [1024], replicated
- loss_mask: int32 [1024], replicated, may hold values 0 or 1
- beam_lengths: int32 [128], replicated, may hold values from 1 to 24, 1024 in all
- beam_group: int32 [128], replicated, may hold values from 0 to 1, as said below
- rewards: float32 [128], replicated, may hold values from 0 to 1, as said below
Outputs:
- logprob: float32 [1024], replicated
- total_loss: float32 [], replicated
- head_grad: bfloat16 [81920, 8192], P(('grp', 'vocab'))
Inputs may be any that keep to these rules, and one draw needn't show every extreme that they name: `beam_group`: each of the 2 groups is named by exactly 64 beams. `rewards`: multiples of 1/8.
All inputs are finite; a program needn't handle non-finite values.
Results may differ from a plain program's by a relative error of at most 0.005.
Values may be sent and summed in bfloat16 or wider, within the bound.
No kernel may reach another device: no remote copies, remote signals or barrier semaphores. Data moves between devices by JAX's collectives and lax.ppermute only.
A program may use at most 128 MiB of HBM per device.

v0:
```python
import jax
import jax.numpy as jnp
from jax import lax
from jax.sharding import PartitionSpec as P

GROUP_BEAMS = 64


def policy_terms(logprob, old_logprobs, loss_mask, beam_lengths, beam_group, rewards):
    highest = lax.Precision.HIGHEST
    tok_count = logprob.shape[0]
    beam_count = beam_lengths.shape[0]
    group_count = beam_count // GROUP_BEAMS
    beam_ends = jnp.cumsum(beam_lengths)
    position = jnp.arange(tok_count, dtype=jnp.int32)
    beam_of = jnp.sum((position[:, None] >= beam_ends[None, :]).astype(jnp.int32), axis=1)
    token_beam = (beam_of[:, None] == jnp.arange(beam_count, dtype=jnp.int32)[None, :]).astype(
        jnp.float32
    )
    beam_onehot = (beam_group[:, None] == jnp.arange(group_count, dtype=jnp.int32)[None, :]).astype(
        jnp.float32
    )
    group_mean = jnp.dot(rewards, beam_onehot, precision=highest) / GROUP_BEAMS
    centred = rewards - jnp.dot(beam_onehot, group_mean, precision=highest)
    group_var = jnp.dot(centred * centred, beam_onehot, precision=highest) / GROUP_BEAMS
    advantage = centred / jnp.sqrt(jnp.dot(beam_onehot, group_var, precision=highest) + 1e-06)
    weight = loss_mask.astype(jnp.float32)
    counts = jnp.dot(weight, token_beam, precision=highest)
    token_adv = jnp.dot(token_beam, advantage, precision=highest)
    token_norm = jnp.dot(token_beam, jnp.maximum(counts, 1.0), precision=highest)
    ratios = jnp.exp(logprob - old_logprobs)
    clipped = jnp.clip(ratios, 0.8, 1.2)
    plain_term = ratios * token_adv
    bounded = clipped * token_adv
    token_share = weight / token_norm
    total_loss = -jnp.sum(token_share * jnp.minimum(plain_term, bounded))
    slopes = -token_share * jnp.where(plain_term <= bounded, plain_term, 0.0)
    return (total_loss, slopes)


def combine(mine, theirs):
    top = jnp.maximum(mine[0], theirs[0])
    total = mine[1] * jnp.exp(mine[0] - top) + theirs[1] * jnp.exp(theirs[0] - top)
    return jnp.stack([top, total, mine[2] + theirs[2]])


def butterfly(stats):
    for axis in ("vocab", "grp"):
        size = lax.axis_size(axis)
        step = 1
        while step < size:
            perm = [(i, i ^ step) for i in range(size)]
            stats = combine(stats, lax.ppermute(stats, axis, perm))
            step *= 2
    return (stats[0], stats[1], stats[2])


def shards(
    hidden, head_weight, targets, old_logprobs, loss_mask, beam_lengths, beam_group, rewards
):
    token_block = lax.all_gather(hidden, "grp", axis=0, tiled=True)
    features = lax.all_gather(token_block, "vocab", axis=1, tiled=True)
    shard = head_weight.shape[0]
    offset = (lax.axis_index("grp") * lax.axis_size("vocab") + lax.axis_index("vocab")) * shard
    vocab_ids = offset + jnp.arange(shard, dtype=jnp.int32)
    logits = lax.dot_general(
        features, head_weight, (((1,), (1,)), ((), ())), preferred_element_type=jnp.float32
    )
    hits = targets[:, None] == vocab_ids[None, :]
    picked = jnp.sum(jnp.where(hits, logits, 0.0), axis=1)
    local_top = jnp.max(logits, axis=1)
    local_sum = jnp.sum(jnp.exp(logits - local_top[:, None]), axis=1)
    top, total, target_logit = butterfly(jnp.stack([local_top, local_sum, picked]))
    log_total = top + jnp.log(total)
    logprob = target_logit - log_total
    total_loss, slopes = policy_terms(
        logprob, old_logprobs, loss_mask, beam_lengths, beam_group, rewards
    )
    grads = (
        slopes[:, None] * (hits.astype(jnp.float32) - jnp.exp(logits - log_total[:, None]))
    ).astype(jnp.bfloat16)
    head_grad = lax.dot_general(
        grads, features, (((0,), (0,)), ((), ())), preferred_element_type=jnp.float32
    )
    return (logprob, total_loss, head_grad.astype(jnp.bfloat16))


def solution(mesh):
    in_specs = (P("grp", "vocab"), P(("grp", "vocab"), None), P(), P(), P(), P(), P(), P())
    out_specs = (P(), P(), P(("grp", "vocab"), None))
    return jax.shard_map(shards, mesh=mesh, in_specs=in_specs, out_specs=out_specs, check_vma=False)
```

profile of v0, /device:TPU:0, one launch (start us, length us, event | category | flops | bytes accessed | tf_op | source)
XLA Modules:
  0.0 226.4 jit_solution(9675438265571959442)
XLA Ops:
  7.2 0.0 all-gather.3.cloned.1.call-start
  7.2 0.7 all-gather.3.cloned.1.call-update
  7.9 0.0 all-gather.5.cloned.1.call-start
  7.9 51.4 %all-gather.3.cloned.1.call-done = bf16[1024,512]{1,0:T(8,128)(2,1)} async-done(((bf16[128,512]{1,0:T(8,128)(2,1)}), bf16[1024,512]{1,0:T(8,128)(2,1)}) %all-gather.3.cloned.1.call-update) | async-done | bytes 1048592 | tf_op jit(solution)/shard_map/all_gather | solution.py:61
  59.3 0.0 all-gather.5.cloned.1.call-update
  59.3 0.7 convert_element_type.17
  60.0 0.8 copy.13
  60.8 0.2 reduce-window.8
  60.9 0.1 reduce
  61.1 0.2 convert_reduce_fusion
  61.3 0.0 copy-start.3
  61.3 90.0 %all-gather.5.cloned.1.call-done = bf16[1024,8192]{1,0:T(8,128)(2,1)} async-done(((bf16[1024,512]{1,0:T(8,128)(2,1)}), bf16[1024,8192]{1,0:T(8,128)(2,1)}) %all-gather.5.cloned.1.call-update) | async-done | bytes 16777232 | tf_op jit(solution)/shard_map/all_gather | solution.py:62
  151.3 16.3 %fusion.53 = (f32[1024]{0:T(1024)S(1)}, f32[1024,640]{0,1:T(8,128)S(1)}) fusion(bf16[1024,8192]{1,0:T(8,128)(2,1)} %all-gather.5.cloned.1.call-done, bf16[640,8192]{1,0:T(8,128)(2,1)} %param.9), kind=kOutput, calls=%fused_computation.105 | convolution fusion | flops 10738072576 | bytes 29888512 | tf_op jit(solution)/shard_map/dot_general | solution.py:66
  167.6 0.0 copy-start.4
  167.6 0.0 copy-start.5
  167.6 0.0 copy-start
  167.6 0.0 copy-start.1
  167.6 0.0 copy-done.3
  167.6 0.6 exponential_reduce_fusion
  168.3 0.3 collective-permute-start
  168.6 0.4 fusion.19
  169.0 0.6 collective-permute-done
  169.6 1.4 collective-permute-start.1
  171.0 0.4 fusion.21
  171.4 2.0 collective-permute-done.1
  173.5 1.6 collective-permute-start.2
  175.1 0.0 copy-done.4
  175.1 0.0 copy-done.5
  175.1 0.2 fusion.15
  175.3 2.1 collective-permute-done.2
  177.4 2.8 %collective-permute-start.3 = (f32[3,1024]{1,0:T(4,128)S(1)}, f32[3,1024]{1,0:T(4,128)S(1)}, u32[]{:S(2)}, u32[]{:S(2)}) collective-permute-start(f32[3,1024]{1,0:T(4,128)S(1)} %pad_maximum_fusion.3), channel_id=1, source_target_pairs={{0,8},{1,9},{2,10},{3,11},{4,12},{5,13},{6,14},{7,15},{8,0},{9,1},... | collective-permute-start | bytes 36872 | tf_op jit(solution)/shard_map/ppermute | solution.py:53
  180.2 0.2 fusion.13
  180.4 2.3 %collective-permute-done.3 = f32[3,1024]{1,0:T(4,128)S(1)} collective-permute-done((f32[3,1024]{1,0:T(4,128)S(1)}, f32[3,1024]{1,0:T(4,128)S(1)}, u32[]{:S(2)}, u32[]{:S(2)}) %collective-permute-start.3) | collective-permute-done | bytes 12320 | tf_op jit(solution)/shard_map/ppermute | solution.py:53
  182.8 1.6 collective-permute-start.4
  184.4 0.2 fusion.12
  184.6 2.0 collective-permute-done.4
  186.6 3.2 %collective-permute-start.5 = (f32[3,1024]{1,0:T(4,128)S(1)}, f32[3,1024]{1,0:T(4,128)S(1)}, u32[]{:S(2)}, u32[]{:S(2)}) collective-permute-start(f32[3,1024]{1,0:T(4,128)S(1)} %pad_maximum_fusion.5), channel_id=1, source_target_pairs={{0,32},{16,48},{32,0},{48,16},{64,96},{80,112},{96,64},{112,80},{1... | collective-permute-start | bytes 36872 | tf_op jit(solution)/shard_map/ppermute | solution.py:53
  189.9 0.2 fusion.17
  190.1 1.9 collective-permute-done.5
  192.0 3.2 %collective-permute-start.6 = (f32[3,1024]{1,0:T(4,128)S(1)}, f32[3,1024]{1,0:T(4,128)S(1)}, u32[]{:S(2)}, u32[]{:S(2)}) collective-permute-start(f32[3,1024]{1,0:T(4,128)S(1)} %pad_maximum_fusion.6), channel_id=1, source_target_pairs={{0,64},{16,80},{32,96},{48,112},{64,0},{80,16},{96,32},{112,48},{1... | collective-permute-start | bytes 36872 | tf_op jit(solution)/shard_map/ppermute | solution.py:53
  195.2 0.4 fusion.20
  195.7 1.8 collective-permute-done.6
  197.5 0.0 copy-done
  197.5 0.0 copy-done.1
  197.5 0.1 fusion.29
  197.6 0.0 copy-start.2
  197.6 0.6 multiply_reduce_fusion
  198.9 19.5 %convolution_convert_fusion = bf16[640,8192]{1,0:T(8,128)(2,1)} fusion(bf16[1024,8192]{1,0:T(8,128)(2,1)} %all-gather.5.cloned.1.call-done, f32[1024,640]{0,1:T(8,128)S(1)} %get-tuple-element.58, f32[1024]{0:T(1024)S(1)} %get-tuple-element.7, f32[1024]{0:T(1024)S(1)} %get-tuple-element.5, s32[1024]{0:T(1024)S(1)} %copy-done.3, s32[640]{0:T(1024)S(1)} %iota_add_fusion), kind=kOutput, calls=%fused_computation | convolution fusion | flops 10746593280 | bytes 29899264 | tf_op jit(solution)/shard_map/dot_general | solution.py:82
  218.4 0.0 copy-done.2
  (15 shorter events, 0.3 us)
Async XLA Ops:
  7.2 52.1 %all-gather.3.cloned.1.call-start = ((), (), s32[]{:S(2)}) async-start(), calls=%async_computation | async-start | bytes 1179648 | tf_op jit(solution)/shard_map/all_gather | solution.py:61
  7.9 143.4 %all-gather.5.cloned.1.call-start = ((), (), s32[]{:S(2)}) async-start(), calls=%async_computation.1 | async-start | bytes 17825792 | tf_op jit(solution)/shard_map/all_gather | solution.py:62
  61.3 106.3 %copy-start.3 = (s32[1024]{0:T(1024)S(1)}, s32[1024]{0:T(1024)}, u32[]{:S(2)}) copy-start(s32[1024]{0:T(1024)} %param.10) | copy-start | bytes 12292
  167.6 7.5 %copy-start.4 = (f32[128]{0:T(128)S(1)}, f32[128]{0:T(128)}, u32[]{:S(2)}) copy-start(f32[128]{0:T(128)} %param.15) | copy-start | bytes 1540
  167.6 7.5 %copy-start.5 = (s32[128]{0:T(128)S(1)}, s32[128]{0:T(128)}, u32[]{:S(2)}) copy-start(s32[128]{0:T(128)} %param.14) | copy-start | bytes 1540
  167.6 29.9 %copy-start = (s32[1024]{0:T(1024)S(1)}, s32[1024]{0:T(1024)}, u32[]{:S(2)}) copy-start(s32[1024]{0:T(1024)} %param.12) | copy-start | bytes 12292
  167.6 29.9 %copy-start.1 = (f32[1024]{0:T(1024)S(1)}, f32[1024]{0:T(1024)}, u32[]{:S(2)}) copy-start(f32[1024]{0:T(1024)} %param.11) | copy-start | bytes 12292
  168.3 1.3 collective-permute-start
  169.6 3.8 %collective-permute-start.1 = (f32[3,1024]{1,0:T(4,128)S(1)}, f32[3,1024]{1,0:T(4,128)S(1)}, u32[]{:S(2)}, u32[]{:S(2)}) collective-permute-start(f32[3,1024]{1,0:T(4,128)S(1)} %pad_maximum_fusion.1), channel_id=1, source_target_pairs={{0,2},{1,3},{2,0},{3,1},{4,6},{5,7},{6,4},{7,5},{8,10},{9,11},{10,... | collective-permute-start | bytes 36872 | tf_op jit(solution)/shard_map/ppermute | solution.py:53
  173.5 3.8 %collective-permute-start.2 = (f32[3,1024]{1,0:T(4,128)S(1)}, f32[3,1024]{1,0:T(4,128)S(1)}, u32[]{:S(2)}, u32[]{:S(2)}) collective-permute-start(f32[3,1024]{1,0:T(4,128)S(1)} %pad_maximum_fusion.2), channel_id=1, source_target_pairs={{0,4},{1,5},{2,6},{3,7},{4,0},{5,1},{6,2},{7,3},{8,12},{9,13},{10,... | collective-permute-start | bytes 36872 | tf_op jit(solution)/shard_map/ppermute | solution.py:53
  177.4 5.3 %collective-permute-start.3 = (f32[3,1024]{1,0:T(4,128)S(1)}, f32[3,1024]{1,0:T(4,128)S(1)}, u32[]{:S(2)}, u32[]{:S(2)}) collective-permute-start(f32[3,1024]{1,0:T(4,128)S(1)} %pad_maximum_fusion.3), channel_id=1, source_target_pairs={{0,8},{1,9},{2,10},{3,11},{4,12},{5,13},{6,14},{7,15},{8,0},{9,1},... | collective-permute-start | bytes 36872 | tf_op jit(solution)/shard_map/ppermute | solution.py:53
  182.8 3.8 %collective-permute-start.4 = (f32[3,1024]{1,0:T(4,128)S(1)}, f32[3,1024]{1,0:T(4,128)S(1)}, u32[]{:S(2)}, u32[]{:S(2)}) collective-permute-start(f32[3,1024]{1,0:T(4,128)S(1)} %pad_maximum_fusion.4), channel_id=1, source_target_pairs={{0,16},{16,0},{32,48},{48,32},{64,80},{80,64},{96,112},{112,96},{1... | collective-permute-start | bytes 36872 | tf_op jit(solution)/shard_map/ppermute | solution.py:53
  186.6 5.3 %collective-permute-start.5 = (f32[3,1024]{1,0:T(4,128)S(1)}, f32[3,1024]{1,0:T(4,128)S(1)}, u32[]{:S(2)}, u32[]{:S(2)}) collective-permute-start(f32[3,1024]{1,0:T(4,128)S(1)} %pad_maximum_fusion.5), channel_id=1, source_target_pairs={{0,32},{16,48},{32,0},{48,16},{64,96},{80,112},{96,64},{112,80},{1... | collective-permute-start | bytes 36872 | tf_op jit(solution)/shard_map/ppermute | solution.py:53
  192.0 5.5 %collective-permute-start.6 = (f32[3,1024]{1,0:T(4,128)S(1)}, f32[3,1024]{1,0:T(4,128)S(1)}, u32[]{:S(2)}, u32[]{:S(2)}) collective-permute-start(f32[3,1024]{1,0:T(4,128)S(1)} %pad_maximum_fusion.6), channel_id=1, source_target_pairs={{0,64},{16,80},{32,96},{48,112},{64,0},{80,16},{96,32},{112,48},{1... | collective-permute-start | bytes 36872 | tf_op jit(solution)/shard_map/ppermute | solution.py:53
  197.6 20.8 %copy-start.2 = (f32[1024]{0:T(1024)}, f32[1024]{0:T(1024)S(1)}, u32[]{:S(2)}) copy-start(f32[1024]{0:T(1024)S(1)} %get-tuple-element.6) | copy-start | bytes 12292
Sparse Core Ops, SparseCore 0:
  10.3 48.9 all-gather.2
  61.0 90.2 all-gather.4
where the time goes:
time: 227 us; the launch traced here: 226 us
  waiting for transfers between devices  155 us (68%)
  matrix products  37.8 us (17%)
  between operations  16 us (7%)
  starting transfers between devices  14.3 us (6%)
  other arithmetic  2.78 us (1%)
    all_gather x1, waiting for transfers between devices, shards(): features = lax.all_gather(token_block, 'vocab', axis=1, tiled=True)  90 us
    all_gather x1, waiting for transfers between devices, shards(): token_block = lax.all_gather(hidden, 'grp', axis=0, tiled=True)  51.4 us
    dot_general x1, matrix products, shards(): lax.dot_general(grads, features, (((0,), (0,)), ((), ())), preferred_elem...  19.5 us
    dot_general x1, matrix products, shards(): lax.dot_general(features, head_weight, (((1,), (1,)), ((), ())), preferre...  16.3 us
    ppermute x7, starting transfers between devices, butterfly(): stats = combine(stats, lax.ppermute(stats, axis, perm))  14.2 us
    ppermute x7, waiting for transfers between devices, butterfly(): stats = combine(stats, lax.ppermute(stats, axis, perm))  12.7 us
  transfers between devices with their start and end apart: 9, of which 9 were waited for; matrix products, arithmetic and copies ran while one was open for 2% of the time, Pallas kernels for 0%

commit v1 on v0

--- a/solution.py
+++ b/solution.py
@@ -58,7 +58,9 @@
 def shards(
     hidden, head_weight, targets, old_logprobs, loss_mask, beam_lengths, beam_group, rewards
 ):
-    token_block = lax.all_gather(hidden, "grp", axis=0, tiled=True)
+    token_block = jnp.concatenate(
+        lax.all_to_all(jnp.stack([hidden] * lax.axis_size("grp")), "grp", 0, 0), axis=0
+    )
     features = lax.all_gather(token_block, "vocab", axis=1, tiled=True)
     shard = head_weight.shape[0]
     offset = (lax.axis_index("grp") * lax.axis_size("vocab") + lax.axis_index("vocab")) * shard

time: 227 us -> 198 us (0.87)
  waiting for transfers between devices: 155 us -> 101 us
  blocking collectives: 0 us -> 24.9 us
    all_gather x1 -> x0, waiting for transfers between devices: 51.4 us -> none  [shards(): token_block = lax.all_gather(hidden, 'grp', axis=0, tiled=True)]
    all_to_all x0 -> x1, blocking collectives: none -> 24.9 us  [shards(): lax.all_to_all(jnp.stack([hidden] * lax.axis_size('grp')), 'grp', 0, 0)]
  transfers between devices with their start and end apart: 9 -> 8, of which waited for: 9 -> 8; matrix products, arithmetic and copies ran while one was open for 2% -> 1% of each run, Pallas kernels for 0% -> 0%
where the time goes in v1:
time: 198 us; the launch traced here: 197 us
  waiting for transfers between devices  101 us (51%)
  matrix products  37.8 us (19%)
  blocking collectives  24.9 us (13%)
  between operations  16 us (8%)
  starting transfers between devices  14.2 us (7%)
  other arithmetic  2.09 us (1%)
    all_gather x1, waiting for transfers between devices, shards(): features = lax.all_gather(token_block, 'vocab', axis=1, tiled=True)  88.4 us
    all_to_all x1, blocking collectives, shards(): lax.all_to_all(jnp.stack([hidden] * lax.axis_size('grp')), 'grp', 0, 0)  24.9 us
    dot_general x1, matrix products, shards(): lax.dot_general(grads, features, (((0,), (0,)), ((), ())), preferred_elem...  19.5 us
    dot_general x1, matrix products, shards(): lax.dot_general(features, head_weight, (((1,), (1,)), ((), ())), preferre...  16.3 us
    ppermute x7, starting transfers between devices, butterfly(): stats = combine(stats, lax.ppermute(stats, axis, perm))  14.2 us
    ppermute x7, waiting for transfers between devices, butterfly(): stats = combine(stats, lax.ppermute(stats, axis, perm))  12.7 us
  transfers between devices with their start and end apart: 8, of which 8 were waited for; matrix products, arithmetic and copies ran while one was open for 1% of the time, Pallas kernels for 0%

profile of v1, /device:TPU:0, one launch (start us, length us, event | category | flops | bytes accessed | tf_op | source)
XLA Modules:
  0.0 197.3 jit_solution(12240403941656959560)
XLA Ops:
  7.2 0.0 copy-start
  7.2 0.0 copy-start.4
  7.2 0.0 all-gather.2.cloned.1.call-start
  7.2 1.0 stack.22
  8.2 24.9 %all_to_all.5 = bf16[8,128,512]{2,1,0:T(8,128)(2,1)} all-to-all(bf16[8,128,512]{2,1,0:T(8,128)(2,1)S(1)} %stack.22), channel_id=1, replica_groups=mesh['grp'=8,'vocab'=16] {'grp'}, dimensions={0} | all-to-all | bytes 2097152 | tf_op jit(solution)/shard_map/all_to_all | solution.py:62
  33.2 0.0 all-gather.2.cloned.1.call-update
  33.2 0.0 copy-done
  33.2 0.0 copy-done.4
  33.2 0.1 copy.13
  33.3 0.2 reduce-window.8
  33.5 0.1 reduce
  33.6 0.2 convert_reduce_fusion
  33.8 0.0 copy-start.3
  33.9 88.4 %all-gather.2.cloned.1.call-done = bf16[1024,8192]{1,0:T(8,128)(2,1)} async-done(((bf16[1024,512]{1,0:T(8,128)(2,1)}), bf16[1024,8192]{1,0:T(8,128)(2,1)}) %all-gather.2.cloned.1.call-update) | async-done | bytes 16777232 | tf_op jit(solution)/shard_map/all_gather | solution.py:64
  122.3 16.3 %fusion.53 = (f32[1024]{0:T(1024)S(1)}, f32[1024,640]{0,1:T(8,128)S(1)}) fusion(bf16[1024,8192]{1,0:T(8,128)(2,1)} %all-gather.2.cloned.1.call-done, bf16[640,8192]{1,0:T(8,128)(2,1)} %param.9), kind=kOutput, calls=%fused_computation.105 | convolution fusion | flops 10738072576 | bytes 29888512 | tf_op jit(solution)/shard_map/dot_general | solution.py:68
  138.6 0.0 copy-start.5
  138.6 0.0 copy-start.6
  138.6 0.0 copy-start.1
  138.6 0.0 copy-done.3
  138.6 0.6 exponential_reduce_fusion
  139.3 0.3 collective-permute-start
  139.6 0.4 fusion.19
  140.0 0.6 collective-permute-done
  140.6 1.4 collective-permute-start.1
  142.0 0.4 fusion.21
  142.4 2.0 %collective-permute-done.1 = f32[3,1024]{1,0:T(4,128)S(1)} collective-permute-done((f32[3,1024]{1,0:T(4,128)S(1)}, f32[3,1024]{1,0:T(4,128)S(1)}, u32[]{:S(2)}, u32[]{:S(2)}) %collective-permute-start.1) | collective-permute-done | bytes 12320 | tf_op jit(solution)/shard_map/ppermute | solution.py:53
  144.5 1.6 collective-permute-start.2
  146.0 0.0 copy-done.5
  146.0 0.0 copy-done.6
  146.0 0.2 fusion.15
  146.2 2.1 %collective-permute-done.2 = f32[3,1024]{1,0:T(4,128)S(1)} collective-permute-done((f32[3,1024]{1,0:T(4,128)S(1)}, f32[3,1024]{1,0:T(4,128)S(1)}, u32[]{:S(2)}, u32[]{:S(2)}) %collective-permute-start.2) | collective-permute-done | bytes 12320 | tf_op jit(solution)/shard_map/ppermute | solution.py:53
  148.3 2.8 %collective-permute-start.3 = (f32[3,1024]{1,0:T(4,128)S(1)}, f32[3,1024]{1,0:T(4,128)S(1)}, u32[]{:S(2)}, u32[]{:S(2)}) collective-permute-start(f32[3,1024]{1,0:T(4,128)S(1)} %pad_maximum_fusion.3), channel_id=1, source_target_pairs={{0,8},{1,9},{2,10},{3,11},{4,12},{5,13},{6,14},{7,15},{8,0},{9,1},... | collective-permute-start | bytes 36872 | tf_op jit(solution)/shard_map/ppermute | solution.py:53
  151.1 0.2 fusion.13
  151.3 2.3 %collective-permute-done.3 = f32[3,1024]{1,0:T(4,128)S(1)} collective-permute-done((f32[3,1024]{1,0:T(4,128)S(1)}, f32[3,1024]{1,0:T(4,128)S(1)}, u32[]{:S(2)}, u32[]{:S(2)}) %collective-permute-start.3) | collective-permute-done | bytes 12320 | tf_op jit(solution)/shard_map/ppermute | solution.py:53
  153.7 1.6 collective-permute-start.4
  155.4 0.2 fusion.12
  155.5 2.0 %collective-permute-done.4 = f32[3,1024]{1,0:T(4,128)S(1)} collective-permute-done((f32[3,1024]{1,0:T(4,128)S(1)}, f32[3,1024]{1,0:T(4,128)S(1)}, u32[]{:S(2)}, u32[]{:S(2)}) %collective-permute-start.4) | collective-permute-done | bytes 12320 | tf_op jit(solution)/shard_map/ppermute | solution.py:53
  157.6 3.2 %collective-permute-start.5 = (f32[3,1024]{1,0:T(4,128)S(1)}, f32[3,1024]{1,0:T(4,128)S(1)}, u32[]{:S(2)}, u32[]{:S(2)}) collective-permute-start(f32[3,1024]{1,0:T(4,128)S(1)} %pad_maximum_fusion.5), channel_id=1, source_target_pairs={{0,32},{16,48},{32,0},{48,16},{64,96},{80,112},{96,64},{112,80},{1... | collective-permute-start | bytes 36872 | tf_op jit(solution)/shard_map/ppermute | solution.py:53
  160.8 0.2 fusion.17
  161.0 1.9 collective-permute-done.5
  163.0 3.2 %collective-permute-start.6 = (f32[3,1024]{1,0:T(4,128)S(1)}, f32[3,1024]{1,0:T(4,128)S(1)}, u32[]{:S(2)}, u32[]{:S(2)}) collective-permute-start(f32[3,1024]{1,0:T(4,128)S(1)} %pad_maximum_fusion.6), channel_id=1, source_target_pairs={{0,64},{16,80},{32,96},{48,112},{64,0},{80,16},{96,32},{112,48},{1... | collective-permute-start | bytes 36872 | tf_op jit(solution)/shard_map/ppermute | solution.py:53
  166.2 0.4 fusion.20
  166.7 1.8 collective-permute-done.6
  168.5 0.0 copy-done.1
  168.5 0.1 fusion.29
  168.6 0.0 copy-start.2
  168.6 0.6 multiply_reduce_fusion
  169.8 19.5 %convolution_convert_fusion = bf16[640,8192]{1,0:T(8,128)(2,1)} fusion(bf16[1024,8192]{1,0:T(8,128)(2,1)} %all-gather.2.cloned.1.call-done, f32[1024,640]{0,1:T(8,128)S(1)} %get-tuple-element.58, f32[1024]{0:T(1024)S(1)} %get-tuple-element.7, f32[1024]{0:T(1024)S(1)} %get-tuple-element.5, s32[1024]{0:T(1024)S(1)} %copy-done.3, s32[640]{0:T(1024)S(1)} %iota_add_fusion), kind=kOutput, calls=%fused_computation | convolution fusion | flops 10746593280 | bytes 29899264 | tf_op jit(solution)/shard_map/dot_general | solution.py:84
  189.4 0.0 copy-done.2
  (16 shorter events, 0.3 us)
Async XLA Ops:
  7.2 26.0 %copy-start = (s32[1024]{0:T(1024)S(1)}, s32[1024]{0:T(1024)}, u32[]{:S(2)}) copy-start(s32[1024]{0:T(1024)} %param.12) | copy-start | bytes 12292
  7.2 26.0 %copy-start.4 = (s32[128]{0:T(128)S(1)}, s32[128]{0:T(128)}, u32[]{:S(2)}) copy-start(s32[128]{0:T(128)} %param.13) | copy-start | bytes 1540
  7.2 115.1 %all-gather.2.cloned.1.call-start = ((), (), s32[]{:S(2)}) async-start(), calls=%async_computation.1 | async-start | bytes 17825792 | tf_op jit(solution)/shard_map/all_gather | solution.py:64
  33.8 104.8 %copy-start.3 = (s32[1024]{0:T(1024)S(1)}, s32[1024]{0:T(1024)}, u32[]{:S(2)}) copy-start(s32[1024]{0:T(1024)} %param.10) | copy-start | bytes 12292
  138.6 7.5 %copy-start.5 = (f32[128]{0:T(128)S(1)}, f32[128]{0:T(128)}, u32[]{:S(2)}) copy-start(f32[128]{0:T(128)} %param.15) | copy-start | bytes 1540
  138.6 7.5 %copy-start.6 = (s32[128]{0:T(128)S(1)}, s32[128]{0:T(128)}, u32[]{:S(2)}) copy-start(s32[128]{0:T(128)} %param.14) | copy-start | bytes 1540
  138.6 29.9 %copy-start.1 = (f32[1024]{0:T(1024)S(1)}, f32[1024]{0:T(1024)}, u32[]{:S(2)}) copy-start(f32[1024]{0:T(1024)} %param.11) | copy-start | bytes 12292
  139.3 1.3 collective-permute-start
  140.6 3.8 %collective-permute-start.1 = (f32[3,1024]{1,0:T(4,128)S(1)}, f32[3,1024]{1,0:T(4,128)S(1)}, u32[]{:S(2)}, u32[]{:S(2)}) collective-permute-start(f32[3,1024]{1,0:T(4,128)S(1)} %pad_maximum_fusion.1), channel_id=1, source_target_pairs={{0,2},{1,3},{2,0},{3,1},{4,6},{5,7},{6,4},{7,5},{8,10},{9,11},{10,... | collective-permute-start | bytes 36872 | tf_op jit(solution)/shard_map/ppermute | solution.py:53
  144.5 3.8 %collective-permute-start.2 = (f32[3,1024]{1,0:T(4,128)S(1)}, f32[3,1024]{1,0:T(4,128)S(1)}, u32[]{:S(2)}, u32[]{:S(2)}) collective-permute-start(f32[3,1024]{1,0:T(4,128)S(1)} %pad_maximum_fusion.2), channel_id=1, source_target_pairs={{0,4},{1,5},{2,6},{3,7},{4,0},{5,1},{6,2},{7,3},{8,12},{9,13},{10,... | collective-permute-start | bytes 36872 | tf_op jit(solution)/shard_map/ppermute | solution.py:53
  148.3 5.3 %collective-permute-start.3 = (f32[3,1024]{1,0:T(4,128)S(1)}, f32[3,1024]{1,0:T(4,128)S(1)}, u32[]{:S(2)}, u32[]{:S(2)}) collective-permute-start(f32[3,1024]{1,0:T(4,128)S(1)} %pad_maximum_fusion.3), channel_id=1, source_target_pairs={{0,8},{1,9},{2,10},{3,11},{4,12},{5,13},{6,14},{7,15},{8,0},{9,1},... | collective-permute-start | bytes 36872 | tf_op jit(solution)/shard_map/ppermute | solution.py:53
  153.7 3.8 %collective-permute-start.4 = (f32[3,1024]{1,0:T(4,128)S(1)}, f32[3,1024]{1,0:T(4,128)S(1)}, u32[]{:S(2)}, u32[]{:S(2)}) collective-permute-start(f32[3,1024]{1,0:T(4,128)S(1)} %pad_maximum_fusion.4), channel_id=1, source_target_pairs={{0,16},{16,0},{32,48},{48,32},{64,80},{80,64},{96,112},{112,96},{1... | collective-permute-start | bytes 36872 | tf_op jit(solution)/shard_map/ppermute | solution.py:53
  157.6 5.3 %collective-permute-start.5 = (f32[3,1024]{1,0:T(4,128)S(1)}, f32[3,1024]{1,0:T(4,128)S(1)}, u32[]{:S(2)}, u32[]{:S(2)}) collective-permute-start(f32[3,1024]{1,0:T(4,128)S(1)} %pad_maximum_fusion.5), channel_id=1, source_target_pairs={{0,32},{16,48},{32,0},{48,16},{64,96},{80,112},{96,64},{112,80},{1... | collective-permute-start | bytes 36872 | tf_op jit(solution)/shard_map/ppermute | solution.py:53
  163.0 5.5 %collective-permute-start.6 = (f32[3,1024]{1,0:T(4,128)S(1)}, f32[3,1024]{1,0:T(4,128)S(1)}, u32[]{:S(2)}, u32[]{:S(2)}) collective-permute-start(f32[3,1024]{1,0:T(4,128)S(1)} %pad_maximum_fusion.6), channel_id=1, source_target_pairs={{0,64},{16,80},{32,96},{48,112},{64,0},{80,16},{96,32},{112,48},{1... | collective-permute-start | bytes 36872 | tf_op jit(solution)/shard_map/ppermute | solution.py:53
  168.6 20.8 %copy-start.2 = (f32[1024]{0:T(1024)}, f32[1024]{0:T(1024)S(1)}, u32[]{:S(2)}) copy-start(f32[1024]{0:T(1024)S(1)} %get-tuple-element.6) | copy-start | bytes 12292
Sparse Core Ops, SparseCore 0:
  33.3 88.9 all-gather.1
